TPU v7x, 128 devices: a whole 4x4x4 slice. The times are simulated.
128 devices in a mesh: req: 16 (over z, y), seq: 8 (over x, core).
Axes of the slice: x: 4, y: 4, z: 4, core: 2. Of those that a mesh axis runs over, the one named last changes fastest.
Arguments:
- queries: bfloat16 [32, 48, 8192], P('req', None, 'seq')
- draft_key_value: bfloat16 [32, 48, 2048], P('req', None, 'seq'), may hold values from -6 to 6
- kv_cache: bfloat16 [32, 16384, 2048], P('req', 'seq')
- cache_lengths: int32 [32], P('req'), may hold values from 2 to 16384, as said below
- ancestors: int32 [32, 48, 48], P('req'), may hold values from 0 to 1, as said below
- dealing: int32 [32], replicated, may hold values from 0 to 31, as said below
- accepted_path: int32 [32, 8], P('req'), may hold values from 0 to 47
Outputs:
- verified_context: bfloat16 [1536, 8192], P(('req', 'seq'))
- kept_entries: bfloat16 [32, 8, 2048], P('req', None, 'seq')
Inputs may be any that keep to these rules, and one draw needn't show every extreme that they name: `dealing`: a permutation of the request ids. `cache_lengths`: at least 2 live positions; some slot's cache is full (16384). Each row is the 0/1 indicator of a draft token's ancestors in its tree, the token itself included; token 0 is the root, a token's parent has a lower index.
All inputs are finite; a program needn't handle non-finite values.
Results may differ from a plain program's by a relative error of at most 0.0046.
Values may be sent and summed in bfloat16 or wider, within the bound.
No kernel may reach another device: no remote copies, remote signals or barrier semaphores. Data moves between devices by JAX's collectives and lax.ppermute only.
A program may use at most 128 MiB of HBM per device.

v0:
```python
import jax
import jax.numpy as jnp
from jax import lax
from jax.sharding import PartitionSpec as P

HEAD_WIDTH = 128
BLK = 1024


def online_merge(earlier, later):
    max_a, sum_a, acc_a = earlier
    max_b, sum_b, acc_b = later
    row_max = jnp.maximum(max_a, max_b)
    scale_a = jnp.exp(max_a - row_max)
    scale_b = jnp.exp(max_b - row_max)
    return (
        row_max,
        sum_a * scale_a + sum_b * scale_b,
        acc_a * scale_a[..., None] + acc_b * scale_b[..., None],
    )


def block_terms(grouped, key_rows, values, allowed):
    scores = jnp.einsum(
        "tkgd,skd->tkgs", grouped, key_rows, preferred_element_type=jnp.float32
    ) * HEAD_WIDTH ** (-0.5)
    scores = jnp.where(allowed, scores, jnp.float32(-1e30))
    row_max = jnp.max(scores, axis=-1)
    weights = jnp.where(allowed, jnp.exp(scores - row_max[..., None]), jnp.float32(0.0))
    row_sum = jnp.sum(weights, axis=-1)
    row_acc = jnp.einsum(
        "tkgs,skd->tkgd", weights.astype(jnp.bfloat16), values, preferred_element_type=jnp.float32
    )
    return (row_max, row_sum, row_acc)


def attend(query_rows, cache_rows, draft_rows, length, pos_offset, tree_mask, use_draft, blk_size):
    tree_len = query_rows.shape[0]
    kv_heads = cache_rows.shape[1] // (2 * HEAD_WIDTH)
    groups = query_rows.shape[1] // (HEAD_WIDTH * kv_heads)
    grouped = query_rows.reshape(tree_len, kv_heads, groups, HEAD_WIDTH)
    draft_part = draft_rows.reshape(tree_len, kv_heads, 2, HEAD_WIDTH)
    draft_allowed = jnp.logical_and(tree_mask > 0, use_draft)[:, None, None, :]
    running = block_terms(grouped, draft_part[:, :, 0], draft_part[:, :, 1], draft_allowed)
    blk_count = cache_rows.shape[0] // blk_size

    def body_step(blk_index, state):
        blk_start = blk_index * blk_size

        def absorb(state_in):
            cache_piece = lax.dynamic_slice_in_dim(cache_rows, blk_start, blk_size, 0).reshape(
                blk_size, kv_heads, 2, HEAD_WIDTH
            )
            positions = pos_offset + blk_start + jnp.arange(blk_size, dtype=jnp.int32)
            allowed = (positions < length)[None, None, None, :]
            return online_merge(
                state_in, block_terms(grouped, cache_piece[:, :, 0], cache_piece[:, :, 1], allowed)
            )

        return lax.cond(pos_offset + blk_start < length, absorb, lambda state_in: state_in, state)

    return lax.fori_loop(0, blk_count, body_step, running)


def body(queries, draft_key_value, kv_cache, cache_lengths, ancestors, dealing, accepted_path):
    local_reqs = kv_cache.shape[0]
    tree_len = queries.shape[1]
    picker = (
        accepted_path[:, :, None] == jnp.arange(tree_len, dtype=jnp.int32)[None, None, :]
    ).astype(jnp.bfloat16)
    kept_entries = jnp.einsum(
        "rit,rtc->ric", picker, draft_key_value, preferred_element_type=jnp.float32
    ).astype(jnp.bfloat16)
    every_query, every_draft = (
        lax.all_gather(queries, "req", axis=0, tiled=True),
        lax.all_gather(draft_key_value, "req", axis=0, tiled=True),
    )
    chosen = lax.dynamic_slice_in_dim(dealing, lax.axis_index("req") * local_reqs, local_reqs)
    own_query = jnp.stack(
        [
            lax.dynamic_index_in_dim(every_query, chosen[slot], 0, keepdims=False)
            for slot in range(local_reqs)
        ],
        axis=0,
    )
    own_draft = jnp.stack(
        [
            lax.dynamic_index_in_dim(every_draft, chosen[slot], 0, keepdims=False)
            for slot in range(local_reqs)
        ],
        axis=0,
    )
    seq_count = lax.axis_size("seq")
    full_query, full_draft = (
        lax.all_gather(own_query, "seq", axis=2, tiled=True),
        lax.all_gather(own_draft, "seq", axis=2, tiled=True),
    )
    position = lax.axis_index("seq")
    pos_offset = position * kv_cache.shape[1]
    maxima, sums, partials = ([], [], [])
    for slot_index in range(local_reqs):
        row_max, row_sum, row_acc = attend(
            full_query[slot_index],
            kv_cache[slot_index],
            full_draft[slot_index],
            cache_lengths[slot_index],
            pos_offset,
            ancestors[slot_index],
            position == 0,
            BLK,
        )
        maxima.append(row_max.reshape(tree_len, -1))
        sums.append(row_sum.reshape(tree_len, -1))
        partials.append(row_acc.reshape(tree_len, -1))
    all_max = jnp.concatenate(maxima, axis=0)
    all_sum = jnp.concatenate(sums, axis=0)
    all_acc = jnp.concatenate(partials, axis=0)
    head_count = all_max.shape[1]
    recv_acc, recv_max, recv_sum = (
        lax.all_to_all(all_acc[None], "seq", split_axis=1, concat_axis=0, tiled=True),
        lax.all_to_all(all_max[None], "seq", split_axis=1, concat_axis=0, tiled=True),
        lax.all_to_all(all_sum[None], "seq", split_axis=1, concat_axis=0, tiled=True),
    )
    top_max = jnp.max(recv_max, axis=0)
    factors = jnp.exp(recv_max - top_max[None])
    denominator = jnp.sum(factors * recv_sum, axis=0)
    token_count = recv_acc.shape[1]
    numerator = jnp.sum(
        factors[..., None] * recv_acc.reshape(seq_count, token_count, head_count, HEAD_WIDTH),
        axis=0,
    )
    context = (
        (numerator / denominator[..., None])
        .reshape(token_count, head_count * HEAD_WIDTH)
        .astype(jnp.bfloat16)
    )
    return (context, kept_entries)


def solution(mesh):
    placed = (
        P("req", None, "seq"),
        P("req", None, "seq"),
        P("req", "seq", None),
        P("req"),
        P("req", None, None),
        P(),
        P("req", None),
    )
    return jax.shard_map(
        body,
        mesh=mesh,
        in_specs=placed,
        out_specs=(P(("req", "seq"), None), P("req", None, "seq")),
        check_vma=False,
    )
```

profile of v0, /device:TPU:1, one launch (start us, length us, event | category | flops | bytes accessed | tf_op | source)
XLA Modules:
  0.0 240.3 jit_solution(1700396935020122704)
XLA Ops:
  7.2 0.7 all-gather.3.cloned.1.call-update
  8.0 0.7 dynamic_slice.23
  8.7 0.6 fusion.56
  12.8 23.5 %all_gather.12 = bf16[32,48,256]{2,1,0:T(8,128)(2,1)S(1)} all-gather(bf16[2,48,256]{2,1,0:T(8,128)(2,1)} %param.16), channel_id=1, replica_groups=mesh['req'=16,'seq'=8] {'req'}, dimensions={0}, use_global_device_ids=true | all-gather | bytes 835584 | tf_op jit(solution)/shard_map/all_gather | solution.py:76
  36.4 18.4 %all_gather.13 = bf16[2,48,2048]{2,1,0:T(8,128)(2,1)S(1)} all-gather(bf16[2,48,256]{2,1,0:T(8,128)(2,1)S(1)} %pad_maximum_fusion.1), channel_id=1, replica_groups=mesh['req'=16,'seq'=8] {'seq'}, dimensions={2}, use_global_device_ids=true | all-gather | bytes 442368 | tf_op jit(solution)/shard_map/all_gather | solution.py:96
  54.8 6.8 %all-gather.3.cloned.1.call-done = bf16[32,48,1024]{2,1,0:T(8,128)(2,1)} async-done(((bf16[2,48,1024]{2,1,0:T(8,128)(2,1)}), bf16[32,48,1024]{2,1,0:T(8,128)(2,1)}) %all-gather.3.cloned.1.call-update) | async-done | bytes 3145744 | tf_op jit(solution)/shard_map/all_gather | solution.py:75
  61.6 1.0 constant_dynamic-slice_fusion.3
  62.6 0.7 pad_maximum_fusion
  63.6 12.0 %fusion.51 = (bf16[1,2048,2048]{2,1,0:T(8,128)(2,1)}, bf16[1,2048,2048]{2,1,0:T(8,128)(2,1)}) fusion(bf16[2,2048,2048]{2,1,0:T(8,128)(2,1)} %param.17), kind=kLoop, calls=%fused_computation.96 | loop fusion | bytes 33554432 | tf_op jit(solution)/shard_map/slice | solution.py:104
  75.6 12.4 %copy.107 = bf16[1,2048,2048]{1,2,0:T(8,128)(2,1)} copy(bf16[1,2048,2048]{2,1,0:T(8,128)(2,1)} %get-tuple-element.463) | data formatting | bytes 16777216
  88.2 12.3 %copy.104 = bf16[1,2048,2048]{1,2,0:T(8,128)(2,1)} copy(bf16[1,2048,2048]{2,1,0:T(8,128)(2,1)} %get-tuple-element.462) | data formatting | bytes 16777216
  100.5 0.6 fusion.55
  101.1 1.0 fusion.54
  102.1 0.9 fusion.53
  103.0 1.5 slice_bitcast_fusion.13
  105.2 1.1 fusion.57
  107.2 26.6 %while.35 = (s32[]{:T(128)}, f32[48,8,8]{0,2,1:T(8,128)S(1)}, f32[48,8,8]{0,2,1:T(8,128)S(1)}, f32[48,8,8,128]{3,0,2,1:T(8,128)S(1)}, s32[]{:T(128)}, /*index=5*...) while((s32[]{:T(128)}, f32[48,8,8]{0,2,1:T(8,128)S(1)}, ...), condition=%wide.region_15.16_spmd, body=%wide.region_10.15_spmd.sunk | while | flops 1652701184 | bytes 54502720 | solution.py:62
  107.9 12.6 %conditional.5 = ((f32[48,8,8]{0,2,1:T(8,128)S(1)}, f32[48,8,8]{0,2,1:T(8,128)S(1)}, f32[48,8,8,128]{3,0,2,1:T(8,128)S(1)})) conditional(s32[]{:T(128)} %convert_element_type.58, (f32[48,8,8]{0,2,1:T(8,128)S(1)}, f32[48,8,8]{0,2,1:T(8,128)S(1)}, f32[48,8,8,128]{3,0,2,1:T(8,128)S(1)}) %tuple.103, (s32[]{:T(128)}, s32[]{:T(128)}, s32[]{:T(128)}, ...), branch_computations={%region_11.11_spmd, %region_12.14_spmd} | conditional | flops 1652701184 | bytes 54502488 | solution.py:60
  107.9 0.6 add_compare_fusion.1
  108.6 2.6 %constant_dynamic-slice_fusion.1 = bf16[1024,2048]{0,1:T(8,128)(2,1)S(1)} fusion(bf16[2048,2048]{0,1:T(8,128)(2,1)} %get-tuple-element.338, s32[]{:T(128)S(6)} %select_n.40), kind=kLoop, calls=%fused_computation.42 | loop fusion | bytes 8388612 | tf_op jit(solution)/shard_map/while/body/eval_jaxpr/cond/branch_1_fun/dynamic_slice | solution.py:51
  111.2 2.2 bitcast_reduce_fusion.1
  113.4 3.6 %fusion.18 = f32[48,8,8]{0,2,1:T(8,128)S(1)} fusion(f32[8,1024,48,8]{1,2,3,0:T(8,128)S(1)} %get-tuple-element.461, f32[48,8,8]{0,2,1:T(8,128)S(1)} %get-tuple-element.460, pred[1024]{0:T(1024)(128)(4,1)S(1)} %add_compare_fusion.1), kind=kLoop, calls=%fused_computation.29 | loop fusion | flops 15725568 | bytes 12608512 | tf_op jit(solution)/shard_map/while/body/eval_jaxpr/cond/branch_1_fun/reduce_sum | solution.py:30
  117.1 3.3 %fusion.24 = f32[48,8,8,128]{3,0,2,1:T(8,128)S(1)} fusion(f32[48,8,8,128]{3,0,2,1:T(8,128)S(1)} %get-tuple-element.341, f32[8,1024,48,8]{1,2,3,0:T(8,128)S(1)} %get-tuple-element.461, f32[48,8,8]{0,2,1:T(8,128)S(1)} %get-tuple-element.460, pred[1024]{0:T(1024)(128)(4,1)S(1)} %add_compare_fusion.1, bf16[1024,8,2,128]{0,3,2,1:T(8,128)(2,1)S(1)} %bitcast.166, ...), kind=kOutput, calls=%fused_computation.37 | convolution fusion | flops 822214656 | bytes 17926144 | tf_op jit(solution)/shard_map/while/body/eval_jaxpr/cond/branch_1_fun/tkgs,skd->tkgd/dot_general | solution.py:31
  121.1 12.6 %conditional.5 = ((f32[48,8,8]{0,2,1:T(8,128)S(1)}, f32[48,8,8]{0,2,1:T(8,128)S(1)}, f32[48,8,8,128]{3,0,2,1:T(8,128)S(1)})) conditional(s32[]{:T(128)} %convert_element_type.58, (f32[48,8,8]{0,2,1:T(8,128)S(1)}, f32[48,8,8]{0,2,1:T(8,128)S(1)}, f32[48,8,8,128]{3,0,2,1:T(8,128)S(1)}) %tuple.103, (s32[]{:T(128)}, s32[]{:T(128)}, s32[]{:T(128)}, ...), branch_computations={%region_11.11_spmd, %region_12.14_spmd} | conditional | flops 1652701184 | bytes 54502488 | solution.py:60
  121.1 0.6 add_compare_fusion.1
  121.8 2.6 %constant_dynamic-slice_fusion.1 = bf16[1024,2048]{0,1:T(8,128)(2,1)S(1)} fusion(bf16[2048,2048]{0,1:T(8,128)(2,1)} %get-tuple-element.338, s32[]{:T(128)S(6)} %select_n.40), kind=kLoop, calls=%fused_computation.42 | loop fusion | bytes 8388612 | tf_op jit(solution)/shard_map/while/body/eval_jaxpr/cond/branch_1_fun/dynamic_slice | solution.py:51
  124.4 2.2 bitcast_reduce_fusion.1
  126.6 3.6 %fusion.18 = f32[48,8,8]{0,2,1:T(8,128)S(1)} fusion(f32[8,1024,48,8]{1,2,3,0:T(8,128)S(1)} %get-tuple-element.461, f32[48,8,8]{0,2,1:T(8,128)S(1)} %get-tuple-element.460, pred[1024]{0:T(1024)(128)(4,1)S(1)} %add_compare_fusion.1), kind=kLoop, calls=%fused_computation.29 | loop fusion | flops 15725568 | bytes 12608512 | tf_op jit(solution)/shard_map/while/body/eval_jaxpr/cond/branch_1_fun/reduce_sum | solution.py:30
  130.3 3.3 %fusion.24 = f32[48,8,8,128]{3,0,2,1:T(8,128)S(1)} fusion(f32[48,8,8,128]{3,0,2,1:T(8,128)S(1)} %get-tuple-element.341, f32[8,1024,48,8]{1,2,3,0:T(8,128)S(1)} %get-tuple-element.461, f32[48,8,8]{0,2,1:T(8,128)S(1)} %get-tuple-element.460, pred[1024]{0:T(1024)(128)(4,1)S(1)} %add_compare_fusion.1, bf16[1024,8,2,128]{0,3,2,1:T(8,128)(2,1)S(1)} %bitcast.166, ...), kind=kOutput, calls=%fused_computation.37 | convolution fusion | flops 822214656 | bytes 17926144 | tf_op jit(solution)/shard_map/while/body/eval_jaxpr/cond/branch_1_fun/tkgs,skd->tkgd/dot_general | solution.py:31
  133.9 1.7 copy.83
  135.8 0.5 copy.69
  136.3 1.1 fusion.58
  138.3 26.5 %while.34 = (s32[]{:T(128)}, f32[48,8,8]{0,2,1:T(8,128)S(1)}, f32[48,8,8]{0,2,1:T(8,128)S(1)}, f32[48,8,8,128]{3,0,2,1:T(8,128)S(1)}, s32[]{:T(128)}, /*index=5*...) while((s32[]{:T(128)}, f32[48,8,8]{0,2,1:T(8,128)S(1)}, ...), condition=%wide.region_7.8_spmd, body=%wide.region_2.7_spmd.sunk | while | flops 1652701184 | bytes 54502720 | solution.py:62
  139.0 12.6 %conditional.4 = ((f32[48,8,8]{0,2,1:T(8,128)S(1)}, f32[48,8,8]{0,2,1:T(8,128)S(1)}, f32[48,8,8,128]{3,0,2,1:T(8,128)S(1)})) conditional(s32[]{:T(128)} %convert_element_type.57, (f32[48,8,8]{0,2,1:T(8,128)S(1)}, f32[48,8,8]{0,2,1:T(8,128)S(1)}, f32[48,8,8,128]{3,0,2,1:T(8,128)S(1)}) %tuple.100, (s32[]{:T(128)}, s32[]{:T(128)}, s32[]{:T(128)}, ...), branch_computations={%region_3.3_spmd, %region_4.6_spmd} | conditional | flops 1652701184 | bytes 54502488 | solution.py:60
  139.0 0.6 add_compare_fusion
  139.6 2.6 %constant_dynamic-slice_fusion = bf16[1024,2048]{0,1:T(8,128)(2,1)S(1)} fusion(bf16[2048,2048]{0,1:T(8,128)(2,1)} %get-tuple-element.318, s32[]{:T(128)S(6)} %select_n.36), kind=kLoop, calls=%fused_computation.19 | loop fusion | bytes 8388612 | tf_op jit(solution)/shard_map/while/body/eval_jaxpr/cond/branch_1_fun/dynamic_slice | solution.py:51
  142.3 2.2 bitcast_reduce_fusion
  144.5 3.6 %fusion.3 = f32[48,8,8]{0,2,1:T(8,128)S(1)} fusion(f32[8,1024,48,8]{1,2,3,0:T(8,128)S(1)} %get-tuple-element.459, f32[48,8,8]{0,2,1:T(8,128)S(1)} %get-tuple-element.458, pred[1024]{0:T(1024)(128)(4,1)S(1)} %add_compare_fusion), kind=kLoop, calls=%fused_computation.6 | loop fusion | flops 15725568 | bytes 12608512 | tf_op jit(solution)/shard_map/while/body/eval_jaxpr/cond/branch_1_fun/reduce_sum | solution.py:30
  148.2 3.3 %fusion.9 = f32[48,8,8,128]{3,0,2,1:T(8,128)S(1)} fusion(f32[48,8,8,128]{3,0,2,1:T(8,128)S(1)} %get-tuple-element.321, f32[8,1024,48,8]{1,2,3,0:T(8,128)S(1)} %get-tuple-element.459, f32[48,8,8]{0,2,1:T(8,128)S(1)} %get-tuple-element.458, pred[1024]{0:T(1024)(128)(4,1)S(1)} %add_compare_fusion, bf16[1024,8,2,128]{0,3,2,1:T(8,128)(2,1)S(1)} %bitcast.168, ...), kind=kOutput, calls=%fused_computation.14 | convolution fusion | flops 822214656 | bytes 17926144 | tf_op jit(solution)/shard_map/while/body/eval_jaxpr/cond/branch_1_fun/tkgs,skd->tkgd/dot_general | solution.py:31
  152.2 12.6 %conditional.4 = ((f32[48,8,8]{0,2,1:T(8,128)S(1)}, f32[48,8,8]{0,2,1:T(8,128)S(1)}, f32[48,8,8,128]{3,0,2,1:T(8,128)S(1)})) conditional(s32[]{:T(128)} %convert_element_type.57, (f32[48,8,8]{0,2,1:T(8,128)S(1)}, f32[48,8,8]{0,2,1:T(8,128)S(1)}, f32[48,8,8,128]{3,0,2,1:T(8,128)S(1)}) %tuple.100, (s32[]{:T(128)}, s32[]{:T(128)}, s32[]{:T(128)}, ...), branch_computations={%region_3.3_spmd, %region_4.6_spmd} | conditional | flops 1652701184 | bytes 54502488 | solution.py:60
  152.2 0.6 add_compare_fusion
  152.9 2.6 %constant_dynamic-slice_fusion = bf16[1024,2048]{0,1:T(8,128)(2,1)S(1)} fusion(bf16[2048,2048]{0,1:T(8,128)(2,1)} %get-tuple-element.318, s32[]{:T(128)S(6)} %select_n.36), kind=kLoop, calls=%fused_computation.19 | loop fusion | bytes 8388612 | tf_op jit(solution)/shard_map/while/body/eval_jaxpr/cond/branch_1_fun/dynamic_slice | solution.py:51
  155.5 2.2 bitcast_reduce_fusion
  157.7 3.6 %fusion.3 = f32[48,8,8]{0,2,1:T(8,128)S(1)} fusion(f32[8,1024,48,8]{1,2,3,0:T(8,128)S(1)} %get-tuple-element.459, f32[48,8,8]{0,2,1:T(8,128)S(1)} %get-tuple-element.458, pred[1024]{0:T(1024)(128)(4,1)S(1)} %add_compare_fusion), kind=kLoop, calls=%fused_computation.6 | loop fusion | flops 15725568 | bytes 12608512 | tf_op jit(solution)/shard_map/while/body/eval_jaxpr/cond/branch_1_fun/reduce_sum | solution.py:30
  161.4 3.3 %fusion.9 = f32[48,8,8,128]{3,0,2,1:T(8,128)S(1)} fusion(f32[48,8,8,128]{3,0,2,1:T(8,128)S(1)} %get-tuple-element.321, f32[8,1024,48,8]{1,2,3,0:T(8,128)S(1)} %get-tuple-element.459, f32[48,8,8]{0,2,1:T(8,128)S(1)} %get-tuple-element.458, pred[1024]{0:T(1024)(128)(4,1)S(1)} %add_compare_fusion, bf16[1024,8,2,128]{0,3,2,1:T(8,128)(2,1)S(1)} %bitcast.168, ...), kind=kOutput, calls=%fused_computation.14 | convolution fusion | flops 822214656 | bytes 17926144 | tf_op jit(solution)/shard_map/while/body/eval_jaxpr/cond/branch_1_fun/tkgs,skd->tkgd/dot_general | solution.py:31
  164.8 1.6 copy.82
  166.6 0.6 broadcast.117
  167.2 0.8 reduce.12
  168.0 0.7 reshape.139
  168.7 4.6 %all-to-all-start.2 = ((f32[8,1,768]{2,1,0:T(1,128)}), f32[8,1,768]{2,1,0:T(1,128)S(1)}, u32[]{:S(2)}, u32[]{:S(2)}) async-start(f32[8,1,768]{2,1,0:T(1,128)} %reshape.139), calls=%async_computation.2 | async-start | bytes 49152 | tf_op jit(solution)/shard_map/all_to_all | solution.py:122
  173.3 4.1 %copy_bitcast_fusion = (f32[48,8192]{1,0:T(8,128)S(1)}, f32[48,8192]{1,0:T(8,128)S(1)}) fusion(f32[6,8,64,128]{3,2,1,0:T(8,128)} %bitcast.176, f32[6,8,64,128]{3,2,1,0:T(8,128)} %bitcast.177), kind=kLoop, calls=%fused_computation.48 | loop fusion | bytes 6291456 | tf_op jit(solution)/shard_map/reshape | solution.py:114
  177.5 0.8 reduce.14
  178.4 0.7 reshape.137
  179.0 4.8 %all-to-all-start = ((f32[8,1,768]{2,1,0:T(1,128)}), f32[8,1,768]{2,1,0:T(1,128)S(1)}, u32[]{:S(2)}, u32[]{:S(2)}) async-start(f32[8,1,768]{2,1,0:T(1,128)} %reshape.137), calls=%async_computation | async-start | bytes 49152 | tf_op jit(solution)/shard_map/all_to_all | solution.py:121
  184.1 4.9 %copy.84 = f32[1,96,8192]{2,0,1:T(1,128)} copy(f32[1,96,8192]{2,1,0:T(8,128)S(1)} %maximum_bitcast_fusion) | data formatting | bytes 6291456 | tf_op jit(solution)/shard_map/broadcast_in_dim | solution.py:120
  189.0 4.9 %all-to-all-start.1 = ((f32[1,96,8192]{2,0,1:T(1,128)}), f32[1,96,8192]{2,0,1:T(1,128)S(1)}, u32[]{:S(2)}, u32[]{:S(2)}) async-start(f32[1,96,8192]{2,0,1:T(1,128)} %copy.84), calls=%async_computation.1 | async-start | bytes 6291456 | tf_op jit(solution)/shard_map/all_to_all | solution.py:120
  194.0 0.8 convolution_convert_fusion
  194.8 0.7 reduce.13
  196.1 0.8 bitcast_reduce_fusion.2
  196.9 0.7 reduce.15
  197.8 0.8 bitcast_reduce_fusion.3
  198.6 32.8 %all-to-all-done.1 = f32[1,96,8192]{2,0,1:T(1,128)S(1)} async-done(((f32[1,96,8192]{2,0,1:T(1,128)}), f32[1,96,8192]{2,0,1:T(1,128)S(1)}, u32[]{:S(2)}, u32[]{:S(2)}) %all-to-all-start.1) | async-done | bytes 3145760 | tf_op jit(solution)/shard_map/all_to_all | solution.py:120
  231.4 1.0 multiply_reduce_fusion
  232.6 0.9 copy.116
  (51 shorter events, 4.9 us)
Async XLA Ops:
  7.2 56.3 %copy-start.3 = (s32[2,48,48]{2,1,0:T(8,128)S(1)}, s32[2,48,48]{2,1,0:T(8,128)}, u32[]{:S(2)}) copy-start(s32[2,48,48]{2,1,0:T(8,128)} %param.19) | copy-start | bytes 55300
  7.2 54.4 %all-gather.3.cloned.1.call-start = ((), (), s32[]{:S(2)}) async-start(), calls=%async_computation.3 | async-start | bytes 3342336 | tf_op jit(solution)/shard_map/all_gather | solution.py:75
  7.9 95.1 %all-gather.5.cloned.1.call-start = ((), (), s32[]{:S(2)}) async-start(), calls=%async_computation.4 | async-start | bytes 1769472 | tf_op jit(solution)/shard_map/all_gather | solution.py:95
  88.2 12.3 %copy-start.4 = (s32[2]{0:T(128)S(1)}, s32[2]{0:T(128)}, u32[]{:S(2)}) copy-start(s32[2]{0:T(128)} %param.18) | copy-start | bytes 28
  104.7 2.0 copy-start.1
  133.9 2.4 %copy-start = (bf16[48,8,1,128]{3,2,1,0:T(2,128)(2,1)S(1)}, bf16[48,8,1,128]{3,2,1,0:T(2,128)(2,1)}, u32[]{:S(2)}) copy-start(bf16[48,8,1,128]{3,2,1,0:T(2,128)(2,1)} %get-tuple-element.473) | copy-start | bytes 294916
  168.7 10.3 %all-to-all-start.2 = ((f32[8,1,768]{2,1,0:T(1,128)}), f32[8,1,768]{2,1,0:T(1,128)S(1)}, u32[]{:S(2)}, u32[]{:S(2)}) async-start(f32[8,1,768]{2,1,0:T(1,128)} %reshape.139), calls=%async_computation.2 | async-start | bytes 49152 | tf_op jit(solution)/shard_map/all_to_all | solution.py:122
  179.0 10.0 %all-to-all-start = ((f32[8,1,768]{2,1,0:T(1,128)}), f32[8,1,768]{2,1,0:T(1,128)S(1)}, u32[]{:S(2)}, u32[]{:S(2)}) async-start(f32[8,1,768]{2,1,0:T(1,128)} %reshape.137), calls=%async_computation | async-start | bytes 49152 | tf_op jit(solution)/shard_map/all_to_all | solution.py:121
  189.0 4.9 %copy-start.2 = (bf16[2,48,256]{2,1,0:T(8,128)(2,1)S(1)}, bf16[2,48,256]{2,1,0:T(8,128)(2,1)}, u32[]{:S(2)}) copy-start(bf16[2,48,256]{2,1,0:T(8,128)(2,1)} %param.16) | copy-start | bytes 147460
  189.0 4.9 %copy-start.5 = (s32[2,8]{1,0:T(2,128)S(1)}, s32[2,8]{1,0:T(2,128)}, u32[]{:S(2)}) copy-start(s32[2,8]{1,0:T(2,128)} %param.21) | copy-start | bytes 196
  189.0 42.4 %all-to-all-start.1 = ((f32[1,96,8192]{2,0,1:T(1,128)}), f32[1,96,8192]{2,0,1:T(1,128)S(1)}, u32[]{:S(2)}, u32[]{:S(2)}) async-start(f32[1,96,8192]{2,0,1:T(1,128)} %copy.84), calls=%async_computation.1 | async-start | bytes 6291456 | tf_op jit(solution)/shard_map/all_to_all | solution.py:120
Sparse Core Ops, SparseCore 0:
  10.1 51.4 all-gather.2
  63.9 23.8 all-gather.4
where the time goes:
time: 242 us; the launch traced here: 240 us
  local copies, waits for them, and re-layouts  73 us (30%)
  blocking collectives  42 us (17%)
  waiting for transfers between devices  40.3 us (17%)
  matrix products  26.1 us (11%)
  other arithmetic  23.6 us (10%)
  between operations  18 us (7%)
  starting transfers between devices  14.4 us (6%)
  loops' own time  3.06 us (1%)
    all_to_all x1, waiting for transfers between devices, body(): lax.all_to_all(all_acc[None], 'seq', split_axis=1, concat_axis=0, tiled=T...  32.8 us
    unnamed x24, local copies, waits for them, and re-layouts  29.6 us
    all_gather x1, blocking collectives, body(): lax.all_gather(draft_key_value, 'req', axis=0, tiled=True)  23.5 us
    all_gather x1, blocking collectives, body(): lax.all_gather(own_draft, 'seq', axis=2, tiled=True)  18.4 us
    reduce_sum x6, other arithmetic, block_terms(): row_sum = jnp.sum(weights, axis=-1)  15.4 us
    dot_general x6, matrix products, block_terms(): jnp.einsum('tkgs,skd->tkgd', weights.astype(jnp.bfloat16), values, prefer...  14.4 us
    slice x1, local copies, waits for them, and re-layouts, body(): kv_cache[slot_index]  12 us
    dot_general x6, matrix products, block_terms(): jnp.einsum('tkgd,skd->tkgs', grouped, key_rows, preferred_element_type=jn...  11 us
  transfers between devices with their start and end apart: 5, of which 2 were waited for; matrix products, arithmetic and copies ran while one was open for 23% of the time, Pallas kernels for 0%

commit v1 on v0

--- a/solution.py
+++ b/solution.py
@@ -5,6 +5,22 @@
 
 HEAD_WIDTH = 128
 BLK = 1024
+
+
+def gather_around(x, axis, dim):
+    ways, here, hop = (lax.axis_size(axis), lax.axis_index(axis), x.shape[dim])
+    lengths = [n * ways if d == dim else n for d, n in enumerate(x.shape)]
+    full = lax.dynamic_update_slice_in_dim(jnp.zeros(lengths, x.dtype), x, here * hop, axis=dim)
+    going_up = going_down = x
+    for far in range(1, ways // 2 + 1):
+        going_up = lax.ppermute(going_up, axis, [(d, (d + 1) % ways) for d in range(ways)])
+        full = lax.dynamic_update_slice_in_dim(full, going_up, (here - far) % ways * hop, axis=dim)
+        if 2 * far < ways:
+            going_down = lax.ppermute(going_down, axis, [(d, (d - 1) % ways) for d in range(ways)])
+            full = lax.dynamic_update_slice_in_dim(
+                full, going_down, (here + far) % ways * hop, axis=dim
+            )
+    return full
 
 
 def online_merge(earlier, later):
@@ -72,7 +88,7 @@
         "rit,rtc->ric", picker, draft_key_value, preferred_element_type=jnp.float32
     ).astype(jnp.bfloat16)
     every_query, every_draft = (
-        lax.all_gather(queries, "req", axis=0, tiled=True),
+        gather_around(queries, "req", 0),
         lax.all_gather(draft_key_value, "req", axis=0, tiled=True),
     )
     chosen = lax.dynamic_slice_in_dim(dealing, lax.axis_index("req") * local_reqs, local_reqs)

time: 242 us -> 305 us (1.26)
  starting transfers between devices: 14.4 us -> 56.6 us
  waiting for transfers between devices: 40.3 us -> 59.8 us
    ppermute x0 -> x15, starting transfers between devices: none -> 35.9 us  [the longest x7 33.6 us: gather_around(): lax.ppermute(going_down, axis, [(d, (d - 1) % ways) for d in range(ways)])]
    ppermute x0 -> x15, waiting for transfers between devices: none -> 26.9 us  [the longest x8 26.9 us: gather_around(): lax.ppermute(going_up, axis, [(d, (d + 1) % ways) for d in range(ways)])]
    all_gather x1 -> x0, waiting for transfers between devices: 6.81 us -> none  [body(): lax.all_gather(queries, 'req', axis=0, tiled=True)]
    all_to_all x1, starting transfers between devices: 4.58 us -> 10.9 us  [body(): lax.all_to_all(all_sum[None], 'seq', split_axis=1, concat_axis=0, tiled=T...]
    all_gather x1, blocking collectives: 23.5 us -> 19.7 us  [body(): lax.all_gather(draft_key_value, 'req', axis=0, tiled=True)]
    unnamed x24 -> x26, local copies, waits for them, and re-layouts: 29.6 us -> 29.6 us
  transfers between devices with their start and end apart: 5 -> 19, of which waited for: 2 -> 8; matrix products, arithmetic and copies ran while one was open for 23% -> 20% of each run, Pallas kernels for 0% -> 0%
where the time goes in v1:
time: 305 us; the launch traced here: 303 us
  local copies, waits for them, and re-layouts  75.3 us (25%)
  waiting for transfers between devices  59.8 us (20%)
  starting transfers between devices  56.6 us (19%)
  blocking collectives  39.2 us (13%)
  matrix products  26.1 us (9%)
  other arithmetic  24.6 us (8%)
  between operations  18.5 us (6%)
    ppermute x7, starting transfers between devices, gather_around(): lax.ppermute(going_down, axis, [(d, (d - 1) % ways) for d in range(ways)])  33.6 us
    all_to_all x1, waiting for transfers between devices, body(): lax.all_to_all(all_acc[None], 'seq', split_axis=1, concat_axis=0, tiled=T...  32.9 us
    unnamed x26, local copies, waits for them, and re-layouts  29.6 us
    ppermute x8, waiting for transfers between devices, gather_around(): lax.ppermute(going_up, axis, [(d, (d + 1) % ways) for d in range(ways)])  26.9 us
    all_gather x1, blocking collectives, body(): lax.all_gather(draft_key_value, 'req', axis=0, tiled=True)  19.7 us
    all_gather x1, blocking collectives, body(): lax.all_gather(own_draft, 'seq', axis=2, tiled=True)  19.5 us
    reduce_sum x6, other arithmetic, block_terms(): row_sum = jnp.sum(weights, axis=-1)  15.4 us
    dot_general x6, matrix products, block_terms(): jnp.einsum('tkgs,skd->tkgd', weights.astype(jnp.bfloat16), values, prefer...  14.4 us
  transfers between devices with their start and end apart: 19, of which 8 were waited for; matrix products, arithmetic and copies ran while one was open for 20% of the time, Pallas kernels for 0%

profile of v1, /device:TPU:1, one launch (start us, length us, event | category | flops | bytes accessed | tf_op | source)
XLA Modules:
  0.0 303.1 jit_solution(10884985867232789499)
XLA Ops:
  7.2 2.2 collective-permute-start
  9.4 5.0 %collective-permute-start.1 = (bf16[2,48,1024]{2,1,0:T(8,128)(2,1)}, bf16[2,48,1024]{2,1,0:T(8,128)(2,1)}, u32[]{:S(2)}, u32[]{:S(2)}) collective-permute-start(bf16[2,48,1024]{2,1,0:T(8,128)(2,1)} %param.15), channel_id=1, source_target_pairs={{0,120},{8,0},{16,8},{24,16},{32,24},{40,32},{48,40},{56,48},{64,5... | collective-permute-start | bytes 589832 | tf_op jit(solution)/shard_map/ppermute | solution.py:19
  18.9 19.7 %all_gather.9 = bf16[32,48,256]{2,1,0:T(8,128)(2,1)} all-gather(bf16[2,48,256]{2,1,0:T(8,128)(2,1)S(1)} %copy-done.3), channel_id=1, replica_groups=mesh['req'=16,'seq'=8] {'req'}, dimensions={0}, use_global_device_ids=true | all-gather | bytes 835584 | tf_op jit(solution)/shard_map/all_gather | solution.py:92
  40.0 0.8 constant_dynamic-slice_fusion.5
  41.4 19.5 %all_gather.10 = bf16[2,48,2048]{2,1,0:T(8,128)(2,1)S(1)} all-gather(bf16[2,48,256]{2,1,0:T(8,128)(2,1)} %pad_maximum_fusion.1), channel_id=1, replica_groups=mesh['req'=16,'seq'=8] {'seq'}, dimensions={2}, use_global_device_ids=true | all-gather | bytes 442368 | tf_op jit(solution)/shard_map/all_gather | solution.py:112
  61.0 4.6 %collective-permute-start.3 = (bf16[2,48,1024]{2,1,0:T(8,128)(2,1)}, bf16[2,48,1024]{2,1,0:T(8,128)(2,1)S(1)}, u32[]{:S(2)}, u32[]{:S(2)}) collective-permute-start(bf16[2,48,1024]{2,1,0:T(8,128)(2,1)} %collective-permute-done.1), channel_id=1, source_target_pairs={{0,120},{8,0},{16,8},{24,16},{32,24},{40,32},{48,40},{56,48},{64,5... | collective-permute-start | bytes 589832 | tf_op jit(solution)/shard_map/ppermute | solution.py:19
  65.6 0.9 constant_dynamic-update-slice_fusion.14
  66.6 0.9 constant_dynamic-update-slice_fusion.13
  67.5 3.1 %collective-permute-done.2 = bf16[2,48,1024]{2,1,0:T(8,128)(2,1)S(1)} collective-permute-done((bf16[2,48,1024]{2,1,0:T(8,128)(2,1)}, bf16[2,48,1024]{2,1,0:T(8,128)(2,1)S(1)}, u32[]{:S(2)}, u32[]{:S(2)}) %collective-permute-start.2) | collective-permute-done | bytes 196640 | tf_op jit(solution)/shard_map/ppermute | solution.py:16
  70.7 4.8 %collective-permute-start.5 = (bf16[2,48,1024]{2,1,0:T(8,128)(2,1)S(1)}, bf16[2,48,1024]{2,1,0:T(8,128)(2,1)S(1)}, u32[]{:S(2)}, u32[]{:S(2)}) collective-permute-start(bf16[2,48,1024]{2,1,0:T(8,128)(2,1)S(1)} %collective-permute-done.3), channel_id=1, source_target_pairs={{0,120},{8,0},{16,8},{24,16},{32,24},{40,32},{48,40},{56,48},{64,5... | collective-permute-start | bytes 589832 | tf_op jit(solution)/shard_map/ppermute | solution.py:19
  75.5 3.9 %collective-permute-done.4 = bf16[2,48,1024]{2,1,0:T(8,128)(2,1)S(1)} collective-permute-done((bf16[2,48,1024]{2,1,0:T(8,128)(2,1)S(1)}, bf16[2,48,1024]{2,1,0:T(8,128)(2,1)S(1)}, u32[]{:S(2)}, u32[]{:S(2)}) %collective-permute-start.4) | collective-permute-done | bytes 196640 | tf_op jit(solution)/shard_map/ppermute | solution.py:16
  79.4 4.8 %collective-permute-start.7 = (bf16[2,48,1024]{2,1,0:T(8,128)(2,1)S(1)}, bf16[2,48,1024]{2,1,0:T(8,128)(2,1)S(1)}, u32[]{:S(2)}, u32[]{:S(2)}) collective-permute-start(bf16[2,48,1024]{2,1,0:T(8,128)(2,1)S(1)} %collective-permute-done.5), channel_id=1, source_target_pairs={{0,120},{8,0},{16,8},{24,16},{32,24},{40,32},{48,40},{56,48},{64,5... | collective-permute-start | bytes 589832 | tf_op jit(solution)/shard_map/ppermute | solution.py:19
  84.3 3.0 collective-permute-done.6
  87.3 4.8 %collective-permute-start.9 = (bf16[2,48,1024]{2,1,0:T(8,128)(2,1)S(1)}, bf16[2,48,1024]{2,1,0:T(8,128)(2,1)S(1)}, u32[]{:S(2)}, u32[]{:S(2)}) collective-permute-start(bf16[2,48,1024]{2,1,0:T(8,128)(2,1)S(1)} %collective-permute-done.7), channel_id=1, source_target_pairs={{0,120},{8,0},{16,8},{24,16},{32,24},{40,32},{48,40},{56,48},{64,5... | collective-permute-start | bytes 589832 | tf_op jit(solution)/shard_map/ppermute | solution.py:19
  92.1 3.0 collective-permute-done.8
  95.1 4.8 %collective-permute-start.11 = (bf16[2,48,1024]{2,1,0:T(8,128)(2,1)S(1)}, bf16[2,48,1024]{2,1,0:T(8,128)(2,1)S(1)}, u32[]{:S(2)}, u32[]{:S(2)}) collective-permute-start(bf16[2,48,1024]{2,1,0:T(8,128)(2,1)S(1)} %collective-permute-done.9), channel_id=1, source_target_pairs={{0,120},{8,0},{16,8},{24,16},{32,24},{40,32},{48,40},{56,48},{64,5... | collective-permute-start | bytes 589832 | tf_op jit(solution)/shard_map/ppermute | solution.py:19
  99.9 3.0 collective-permute-done.10
  103.0 4.8 %collective-permute-start.13 = (bf16[2,48,1024]{2,1,0:T(8,128)(2,1)S(1)}, bf16[2,48,1024]{2,1,0:T(8,128)(2,1)S(1)}, u32[]{:S(2)}, u32[]{:S(2)}) collective-permute-start(bf16[2,48,1024]{2,1,0:T(8,128)(2,1)S(1)} %collective-permute-done.11), channel_id=1, source_target_pairs={{0,120},{8,0},{16,8},{24,16},{32,24},{40,32},{48,40},{56,48},{64,5... | collective-permute-start | bytes 589832 | tf_op jit(solution)/shard_map/ppermute | solution.py:19
  107.8 3.0 collective-permute-done.12
  110.8 7.8 %collective-permute-done.14 = bf16[2,48,1024]{2,1,0:T(8,128)(2,1)S(1)} collective-permute-done((bf16[2,48,1024]{2,1,0:T(8,128)(2,1)S(1)}, bf16[2,48,1024]{2,1,0:T(8,128)(2,1)S(1)}, u32[]{:S(2)}, u32[]{:S(2)}) %collective-permute-start.14) | collective-permute-done | bytes 196640 | tf_op jit(solution)/shard_map/ppermute | solution.py:16
  119.6 0.8 fusion.43
  120.5 12.0 %fusion.51 = (bf16[1,2048,2048]{2,1,0:T(8,128)(2,1)}, bf16[1,2048,2048]{2,1,0:T(8,128)(2,1)}) fusion(bf16[2,2048,2048]{2,1,0:T(8,128)(2,1)} %param.17), kind=kLoop, calls=%fused_computation.112 | loop fusion | bytes 33554432 | tf_op jit(solution)/shard_map/slice | solution.py:120
  132.5 12.3 %copy.107 = bf16[1,2048,2048]{1,2,0:T(8,128)(2,1)} copy(bf16[1,2048,2048]{2,1,0:T(8,128)(2,1)} %get-tuple-element.463) | data formatting | bytes 16777216
  145.0 12.4 %copy.104 = bf16[1,2048,2048]{1,2,0:T(8,128)(2,1)} copy(bf16[1,2048,2048]{2,1,0:T(8,128)(2,1)} %get-tuple-element.462) | data formatting | bytes 16777216
  158.0 1.0 fusion.54
  158.9 1.0 fusion.53
  159.9 1.5 slice_bitcast_fusion.13
  162.1 1.1 fusion.57
  164.1 26.4 %while.35 = (s32[]{:T(128)}, f32[48,8,8]{0,2,1:T(8,128)S(1)}, f32[48,8,8]{0,2,1:T(8,128)S(1)}, f32[48,8,8,128]{3,0,2,1:T(8,128)S(1)}, s32[]{:T(128)}, /*index=5*...) while((s32[]{:T(128)}, f32[48,8,8]{0,2,1:T(8,128)S(1)}, ...), condition=%wide.region_15.16_spmd, body=%wide.region_10.15_spmd.sunk | while | flops 1652701184 | bytes 54502720 | solution.py:78
  164.7 12.5 %conditional.5 = ((f32[48,8,8]{0,2,1:T(8,128)S(1)}, f32[48,8,8]{0,2,1:T(8,128)S(1)}, f32[48,8,8,128]{3,0,2,1:T(8,128)S(1)})) conditional(s32[]{:T(128)} %convert_element_type.58, (f32[48,8,8]{0,2,1:T(8,128)S(1)}, f32[48,8,8]{0,2,1:T(8,128)S(1)}, f32[48,8,8,128]{3,0,2,1:T(8,128)S(1)}) %tuple.103, (s32[]{:T(128)}, s32[]{:T(128)}, s32[]{:T(128)}, ...), branch_computations={%region_11.11_spmd, %region_12.14_spmd} | conditional | flops 1652701184 | bytes 54502488 | solution.py:76
  165.3 2.6 constant_dynamic-slice_fusion.1
  167.9 2.2 bitcast_reduce_fusion.1
  170.1 3.6 %fusion.18 = f32[48,8,8]{0,2,1:T(8,128)S(1)} fusion(f32[8,1024,48,8]{1,2,3,0:T(8,128)S(1)} %get-tuple-element.461, f32[48,8,8]{0,2,1:T(8,128)S(1)} %get-tuple-element.460, pred[1024]{0:T(1024)(128)(4,1)S(1)} %add_compare_fusion.1), kind=kLoop, calls=%fused_computation.29 | loop fusion | flops 15725568 | bytes 12608512 | tf_op jit(solution)/shard_map/while/body/eval_jaxpr/cond/branch_1_fun/reduce_sum | solution.py:46
  173.8 3.3 %fusion.24 = f32[48,8,8,128]{3,0,2,1:T(8,128)S(1)} fusion(f32[48,8,8,128]{3,0,2,1:T(8,128)S(1)} %get-tuple-element.341, f32[8,1024,48,8]{1,2,3,0:T(8,128)S(1)} %get-tuple-element.461, f32[48,8,8]{0,2,1:T(8,128)S(1)} %get-tuple-element.460, pred[1024]{0:T(1024)(128)(4,1)S(1)} %add_compare_fusion.1, bf16[1024,8,2,128]{0,3,2,1:T(8,128)(2,1)S(1)} %bitcast.166, ...), kind=kOutput, calls=%fused_computation.37 | convolution fusion | flops 822214656 | bytes 17926144 | tf_op jit(solution)/shard_map/while/body/eval_jaxpr/cond/branch_1_fun/tkgs,skd->tkgd/dot_general | solution.py:47
  177.8 12.5 %conditional.5 = ((f32[48,8,8]{0,2,1:T(8,128)S(1)}, f32[48,8,8]{0,2,1:T(8,128)S(1)}, f32[48,8,8,128]{3,0,2,1:T(8,128)S(1)})) conditional(s32[]{:T(128)} %convert_element_type.58, (f32[48,8,8]{0,2,1:T(8,128)S(1)}, f32[48,8,8]{0,2,1:T(8,128)S(1)}, f32[48,8,8,128]{3,0,2,1:T(8,128)S(1)}) %tuple.103, (s32[]{:T(128)}, s32[]{:T(128)}, s32[]{:T(128)}, ...), branch_computations={%region_11.11_spmd, %region_12.14_spmd} | conditional | flops 1652701184 | bytes 54502488 | solution.py:76
  178.4 2.6 constant_dynamic-slice_fusion.1
  181.0 2.2 bitcast_reduce_fusion.1
  183.2 3.6 %fusion.18 = f32[48,8,8]{0,2,1:T(8,128)S(1)} fusion(f32[8,1024,48,8]{1,2,3,0:T(8,128)S(1)} %get-tuple-element.461, f32[48,8,8]{0,2,1:T(8,128)S(1)} %get-tuple-element.460, pred[1024]{0:T(1024)(128)(4,1)S(1)} %add_compare_fusion.1), kind=kLoop, calls=%fused_computation.29 | loop fusion | flops 15725568 | bytes 12608512 | tf_op jit(solution)/shard_map/while/body/eval_jaxpr/cond/branch_1_fun/reduce_sum | solution.py:46
  186.9 3.3 %fusion.24 = f32[48,8,8,128]{3,0,2,1:T(8,128)S(1)} fusion(f32[48,8,8,128]{3,0,2,1:T(8,128)S(1)} %get-tuple-element.341, f32[8,1024,48,8]{1,2,3,0:T(8,128)S(1)} %get-tuple-element.461, f32[48,8,8]{0,2,1:T(8,128)S(1)} %get-tuple-element.460, pred[1024]{0:T(1024)(128)(4,1)S(1)} %add_compare_fusion.1, bf16[1024,8,2,128]{0,3,2,1:T(8,128)(2,1)S(1)} %bitcast.166, ...), kind=kOutput, calls=%fused_computation.37 | convolution fusion | flops 822214656 | bytes 17926144 | tf_op jit(solution)/shard_map/while/body/eval_jaxpr/cond/branch_1_fun/tkgs,skd->tkgd/dot_general | solution.py:47
  190.5 1.7 copy.83
  192.9 1.1 fusion.58
  194.9 26.4 %while.34 = (s32[]{:T(128)}, f32[48,8,8]{0,2,1:T(8,128)S(1)}, f32[48,8,8]{0,2,1:T(8,128)S(1)}, f32[48,8,8,128]{3,0,2,1:T(8,128)S(1)}, s32[]{:T(128)}, /*index=5*...) while((s32[]{:T(128)}, f32[48,8,8]{0,2,1:T(8,128)S(1)}, ...), condition=%wide.region_7.8_spmd, body=%wide.region_2.7_spmd.sunk | while | flops 1652701184 | bytes 54502720 | solution.py:78
  195.6 12.6 %conditional.4 = ((f32[48,8,8]{0,2,1:T(8,128)S(1)}, f32[48,8,8]{0,2,1:T(8,128)S(1)}, f32[48,8,8,128]{3,0,2,1:T(8,128)S(1)})) conditional(s32[]{:T(128)} %convert_element_type.57, (f32[48,8,8]{0,2,1:T(8,128)S(1)}, f32[48,8,8]{0,2,1:T(8,128)S(1)}, f32[48,8,8,128]{3,0,2,1:T(8,128)S(1)}) %tuple.100, (s32[]{:T(128)}, s32[]{:T(128)}, s32[]{:T(128)}, ...), branch_computations={%region_3.3_spmd, %region_4.6_spmd} | conditional | flops 1652701184 | bytes 54502488 | solution.py:76
  196.3 2.6 constant_dynamic-slice_fusion
  198.9 2.2 bitcast_reduce_fusion
  201.1 3.6 %fusion.3 = f32[48,8,8]{0,2,1:T(8,128)S(1)} fusion(f32[8,1024,48,8]{1,2,3,0:T(8,128)S(1)} %get-tuple-element.459, f32[48,8,8]{0,2,1:T(8,128)S(1)} %get-tuple-element.458, pred[1024]{0:T(1024)(128)(4,1)S(1)} %add_compare_fusion), kind=kLoop, calls=%fused_computation.6 | loop fusion | flops 15725568 | bytes 12608512 | tf_op jit(solution)/shard_map/while/body/eval_jaxpr/cond/branch_1_fun/reduce_sum | solution.py:46
  204.8 3.3 %fusion.9 = f32[48,8,8,128]{3,0,2,1:T(8,128)S(1)} fusion(f32[48,8,8,128]{3,0,2,1:T(8,128)S(1)} %get-tuple-element.321, f32[8,1024,48,8]{1,2,3,0:T(8,128)S(1)} %get-tuple-element.459, f32[48,8,8]{0,2,1:T(8,128)S(1)} %get-tuple-element.458, pred[1024]{0:T(1024)(128)(4,1)S(1)} %add_compare_fusion, bf16[1024,8,2,128]{0,3,2,1:T(8,128)(2,1)S(1)} %bitcast.168, ...), kind=kOutput, calls=%fused_computation.14 | convolution fusion | flops 822214656 | bytes 17926144 | tf_op jit(solution)/shard_map/while/body/eval_jaxpr/cond/branch_1_fun/tkgs,skd->tkgd/dot_general | solution.py:47
  208.8 12.6 %conditional.4 = ((f32[48,8,8]{0,2,1:T(8,128)S(1)}, f32[48,8,8]{0,2,1:T(8,128)S(1)}, f32[48,8,8,128]{3,0,2,1:T(8,128)S(1)})) conditional(s32[]{:T(128)} %convert_element_type.57, (f32[48,8,8]{0,2,1:T(8,128)S(1)}, f32[48,8,8]{0,2,1:T(8,128)S(1)}, f32[48,8,8,128]{3,0,2,1:T(8,128)S(1)}) %tuple.100, (s32[]{:T(128)}, s32[]{:T(128)}, s32[]{:T(128)}, ...), branch_computations={%region_3.3_spmd, %region_4.6_spmd} | conditional | flops 1652701184 | bytes 54502488 | solution.py:76
  209.5 2.6 constant_dynamic-slice_fusion
  212.1 2.2 bitcast_reduce_fusion
  214.3 3.6 %fusion.3 = f32[48,8,8]{0,2,1:T(8,128)S(1)} fusion(f32[8,1024,48,8]{1,2,3,0:T(8,128)S(1)} %get-tuple-element.459, f32[48,8,8]{0,2,1:T(8,128)S(1)} %get-tuple-element.458, pred[1024]{0:T(1024)(128)(4,1)S(1)} %add_compare_fusion), kind=kLoop, calls=%fused_computation.6 | loop fusion | flops 15725568 | bytes 12608512 | tf_op jit(solution)/shard_map/while/body/eval_jaxpr/cond/branch_1_fun/reduce_sum | solution.py:46
  218.0 3.3 %fusion.9 = f32[48,8,8,128]{3,0,2,1:T(8,128)S(1)} fusion(f32[48,8,8,128]{3,0,2,1:T(8,128)S(1)} %get-tuple-element.321, f32[8,1024,48,8]{1,2,3,0:T(8,128)S(1)} %get-tuple-element.459, f32[48,8,8]{0,2,1:T(8,128)S(1)} %get-tuple-element.458, pred[1024]{0:T(1024)(128)(4,1)S(1)} %add_compare_fusion, bf16[1024,8,2,128]{0,3,2,1:T(8,128)(2,1)S(1)} %bitcast.168, ...), kind=kOutput, calls=%fused_computation.14 | convolution fusion | flops 822214656 | bytes 17926144 | tf_op jit(solution)/shard_map/while/body/eval_jaxpr/cond/branch_1_fun/tkgs,skd->tkgd/dot_general | solution.py:47
  221.4 1.6 copy.82
  225.2 10.9 %all-to-all-start.2 = ((f32[8,1,768]{2,1,0:T(1,128)}), f32[8,1,768]{2,1,0:T(1,128)S(1)}, u32[]{:S(2)}, u32[]{:S(2)}) async-start(f32[8,1,768]{2,1,0:T(1,128)} %reshape.139), calls=%async_computation.2 | async-start | bytes 49152 | tf_op jit(solution)/shard_map/all_to_all | solution.py:138
  236.1 4.1 %copy_bitcast_fusion = (f32[48,8192]{1,0:T(8,128)S(1)}, f32[48,8192]{1,0:T(8,128)S(1)}) fusion(f32[6,8,64,128]{3,2,1,0:T(8,128)} %bitcast.176, f32[6,8,64,128]{3,2,1,0:T(8,128)} %bitcast.177), kind=kLoop, calls=%fused_computation.48 | loop fusion | bytes 6291456 | tf_op jit(solution)/shard_map/reshape | solution.py:130
  241.8 4.8 %all-to-all-start = ((f32[8,1,768]{2,1,0:T(1,128)}), f32[8,1,768]{2,1,0:T(1,128)S(1)}, u32[]{:S(2)}, u32[]{:S(2)}) async-start(f32[8,1,768]{2,1,0:T(1,128)} %reshape.137), calls=%async_computation | async-start | bytes 49152 | tf_op jit(solution)/shard_map/all_to_all | solution.py:137
  246.8 4.9 %copy.84 = f32[1,96,8192]{2,0,1:T(1,128)} copy(f32[1,96,8192]{2,1,0:T(8,128)S(1)} %maximum_bitcast_fusion) | data formatting | bytes 6291456 | tf_op jit(solution)/shard_map/broadcast_in_dim | solution.py:136
  251.8 4.9 %all-to-all-start.1 = ((f32[1,96,8192]{2,0,1:T(1,128)}), f32[1,96,8192]{2,0,1:T(1,128)S(1)}, u32[]{:S(2)}, u32[]{:S(2)}) async-start(f32[1,96,8192]{2,0,1:T(1,128)} %copy.84), calls=%async_computation.1 | async-start | bytes 6291456 | tf_op jit(solution)/shard_map/all_to_all | solution.py:136
  256.7 0.8 convolution_convert_fusion
  258.8 0.8 bitcast_reduce_fusion.2
  260.4 0.8 bitcast_reduce_fusion.3
  261.2 32.9 %all-to-all-done.1 = f32[1,96,8192]{2,0,1:T(1,128)S(1)} async-done(((f32[1,96,8192]{2,0,1:T(1,128)}), f32[1,96,8192]{2,0,1:T(1,128)S(1)}, u32[]{:S(2)}, u32[]{:S(2)}) %all-to-all-start.1) | async-done | bytes 3145760 | tf_op jit(solution)/shard_map/all_to_all | solution.py:136
  294.1 1.0 multiply_reduce_fusion
  295.4 0.9 copy.116
  (97 shorter events, 16.8 us)
Async XLA Ops:
  7.2 11.7 %copy-start.2 = (bf16[2,48,1024]{2,1,0:T(8,128)(2,1)S(1)}, bf16[2,48,1024]{2,1,0:T(8,128)(2,1)}, u32[]{:S(2)}) copy-start(bf16[2,48,1024]{2,1,0:T(8,128)(2,1)} %param.15) | copy-start | bytes 589828
  7.2 11.7 %copy-start.3 = (bf16[2,48,256]{2,1,0:T(8,128)(2,1)S(1)}, bf16[2,48,256]{2,1,0:T(8,128)(2,1)}, u32[]{:S(2)}) copy-start(bf16[2,48,256]{2,1,0:T(8,128)(2,1)} %param.16) | copy-start | bytes 147460
  7.2 152.7 %all-gather.2.cloned.1.call-start = ((), (), s32[]{:S(2)}) async-start(), calls=%async_computation.3 | async-start | bytes 1769472 | tf_op jit(solution)/shard_map/all_gather | solution.py:111
  7.2 53.6 %collective-permute-start = (bf16[2,48,1024]{2,1,0:T(8,128)(2,1)}, bf16[2,48,1024]{2,1,0:T(8,128)(2,1)}, u32[]{:S(2)}, u32[]{:S(2)}) collective-permute-start(bf16[2,48,1024]{2,1,0:T(8,128)(2,1)} %param.15), channel_id=1, source_target_pairs={{0,8},{8,16},{16,24},{24,32},{32,40},{40,48},{48,56},{56,64},{64,7... | collective-permute-start | bytes 589832 | tf_op jit(solution)/shard_map/ppermute | solution.py:16
  9.4 51.6 %collective-permute-start.1 = (bf16[2,48,1024]{2,1,0:T(8,128)(2,1)}, bf16[2,48,1024]{2,1,0:T(8,128)(2,1)}, u32[]{:S(2)}, u32[]{:S(2)}) collective-permute-start(bf16[2,48,1024]{2,1,0:T(8,128)(2,1)} %param.15), channel_id=1, source_target_pairs={{0,120},{8,0},{16,8},{24,16},{32,24},{40,32},{48,40},{56,48},{64,5... | collective-permute-start | bytes 589832 | tf_op jit(solution)/shard_map/ppermute | solution.py:19
  60.8 9.8 %collective-permute-start.2 = (bf16[2,48,1024]{2,1,0:T(8,128)(2,1)}, bf16[2,48,1024]{2,1,0:T(8,128)(2,1)S(1)}, u32[]{:S(2)}, u32[]{:S(2)}) collective-permute-start(bf16[2,48,1024]{2,1,0:T(8,128)(2,1)} %collective-permute-done), channel_id=1, source_target_pairs={{0,8},{8,16},{16,24},{24,32},{32,40},{40,48},{48,56},{56,64},{64,7... | collective-permute-start | bytes 589832 | tf_op jit(solution)/shard_map/ppermute | solution.py:16
  61.0 9.7 %collective-permute-start.3 = (bf16[2,48,1024]{2,1,0:T(8,128)(2,1)}, bf16[2,48,1024]{2,1,0:T(8,128)(2,1)S(1)}, u32[]{:S(2)}, u32[]{:S(2)}) collective-permute-start(bf16[2,48,1024]{2,1,0:T(8,128)(2,1)} %collective-permute-done.1), channel_id=1, source_target_pairs={{0,120},{8,0},{16,8},{24,16},{32,24},{40,32},{48,40},{56,48},{64,5... | collective-permute-start | bytes 589832 | tf_op jit(solution)/shard_map/ppermute | solution.py:19
  70.7 8.8 %collective-permute-start.4 = (bf16[2,48,1024]{2,1,0:T(8,128)(2,1)S(1)}, bf16[2,48,1024]{2,1,0:T(8,128)(2,1)S(1)}, u32[]{:S(2)}, u32[]{:S(2)}) collective-permute-start(bf16[2,48,1024]{2,1,0:T(8,128)(2,1)S(1)} %collective-permute-done.2), channel_id=1, source_target_pairs={{0,8},{8,16},{16,24},{24,32},{32,40},{40,48},{48,56},{56,64},{64,7... | collective-permute-start | bytes 589832 | tf_op jit(solution)/shard_map/ppermute | solution.py:16
  70.7 8.8 %collective-permute-start.5 = (bf16[2,48,1024]{2,1,0:T(8,128)(2,1)S(1)}, bf16[2,48,1024]{2,1,0:T(8,128)(2,1)S(1)}, u32[]{:S(2)}, u32[]{:S(2)}) collective-permute-start(bf16[2,48,1024]{2,1,0:T(8,128)(2,1)S(1)} %collective-permute-done.3), channel_id=1, source_target_pairs={{0,120},{8,0},{16,8},{24,16},{32,24},{40,32},{48,40},{56,48},{64,5... | collective-permute-start | bytes 589832 | tf_op jit(solution)/shard_map/ppermute | solution.py:19
  79.4 7.8 %collective-permute-start.6 = (bf16[2,48,1024]{2,1,0:T(8,128)(2,1)S(1)}, bf16[2,48,1024]{2,1,0:T(8,128)(2,1)S(1)}, u32[]{:S(2)}, u32[]{:S(2)}) collective-permute-start(bf16[2,48,1024]{2,1,0:T(8,128)(2,1)S(1)} %collective-permute-done.4), channel_id=1, source_target_pairs={{0,8},{8,16},{16,24},{24,32},{32,40},{40,48},{48,56},{56,64},{64,7... | collective-permute-start | bytes 589832 | tf_op jit(solution)/shard_map/ppermute | solution.py:16
  79.4 7.8 %collective-permute-start.7 = (bf16[2,48,1024]{2,1,0:T(8,128)(2,1)S(1)}, bf16[2,48,1024]{2,1,0:T(8,128)(2,1)S(1)}, u32[]{:S(2)}, u32[]{:S(2)}) collective-permute-start(bf16[2,48,1024]{2,1,0:T(8,128)(2,1)S(1)} %collective-permute-done.5), channel_id=1, source_target_pairs={{0,120},{8,0},{16,8},{24,16},{32,24},{40,32},{48,40},{56,48},{64,5... | collective-permute-start | bytes 589832 | tf_op jit(solution)/shard_map/ppermute | solution.py:19
  87.3 7.8 %collective-permute-start.8 = (bf16[2,48,1024]{2,1,0:T(8,128)(2,1)S(1)}, bf16[2,48,1024]{2,1,0:T(8,128)(2,1)S(1)}, u32[]{:S(2)}, u32[]{:S(2)}) collective-permute-start(bf16[2,48,1024]{2,1,0:T(8,128)(2,1)S(1)} %collective-permute-done.6), channel_id=1, source_target_pairs={{0,8},{8,16},{16,24},{24,32},{32,40},{40,48},{48,56},{56,64},{64,7... | collective-permute-start | bytes 589832 | tf_op jit(solution)/shard_map/ppermute | solution.py:16
  87.3 7.8 %collective-permute-start.9 = (bf16[2,48,1024]{2,1,0:T(8,128)(2,1)S(1)}, bf16[2,48,1024]{2,1,0:T(8,128)(2,1)S(1)}, u32[]{:S(2)}, u32[]{:S(2)}) collective-permute-start(bf16[2,48,1024]{2,1,0:T(8,128)(2,1)S(1)} %collective-permute-done.7), channel_id=1, source_target_pairs={{0,120},{8,0},{16,8},{24,16},{32,24},{40,32},{48,40},{56,48},{64,5... | collective-permute-start | bytes 589832 | tf_op jit(solution)/shard_map/ppermute | solution.py:19
  95.1 7.8 %collective-permute-start.10 = (bf16[2,48,1024]{2,1,0:T(8,128)(2,1)S(1)}, bf16[2,48,1024]{2,1,0:T(8,128)(2,1)S(1)}, u32[]{:S(2)}, u32[]{:S(2)}) collective-permute-start(bf16[2,48,1024]{2,1,0:T(8,128)(2,1)S(1)} %collective-permute-done.8), channel_id=1, source_target_pairs={{0,8},{8,16},{16,24},{24,32},{32,40},{40,48},{48,56},{56,64},{64,7... | collective-permute-start | bytes 589832 | tf_op jit(solution)/shard_map/ppermute | solution.py:16
  95.1 7.8 %collective-permute-start.11 = (bf16[2,48,1024]{2,1,0:T(8,128)(2,1)S(1)}, bf16[2,48,1024]{2,1,0:T(8,128)(2,1)S(1)}, u32[]{:S(2)}, u32[]{:S(2)}) collective-permute-start(bf16[2,48,1024]{2,1,0:T(8,128)(2,1)S(1)} %collective-permute-done.9), channel_id=1, source_target_pairs={{0,120},{8,0},{16,8},{24,16},{32,24},{40,32},{48,40},{56,48},{64,5... | collective-permute-start | bytes 589832 | tf_op jit(solution)/shard_map/ppermute | solution.py:19
  102.9 7.8 %collective-permute-start.12 = (bf16[2,48,1024]{2,1,0:T(8,128)(2,1)S(1)}, bf16[2,48,1024]{2,1,0:T(8,128)(2,1)S(1)}, u32[]{:S(2)}, u32[]{:S(2)}) collective-permute-start(bf16[2,48,1024]{2,1,0:T(8,128)(2,1)S(1)} %collective-permute-done.10), channel_id=1, source_target_pairs={{0,8},{8,16},{16,24},{24,32},{32,40},{40,48},{48,56},{56,64},{64,7... | collective-permute-start | bytes 589832 | tf_op jit(solution)/shard_map/ppermute | solution.py:16
  103.0 7.9 %collective-permute-start.13 = (bf16[2,48,1024]{2,1,0:T(8,128)(2,1)S(1)}, bf16[2,48,1024]{2,1,0:T(8,128)(2,1)S(1)}, u32[]{:S(2)}, u32[]{:S(2)}) collective-permute-start(bf16[2,48,1024]{2,1,0:T(8,128)(2,1)S(1)} %collective-permute-done.11), channel_id=1, source_target_pairs={{0,120},{8,0},{16,8},{24,16},{32,24},{40,32},{48,40},{56,48},{64,5... | collective-permute-start | bytes 589832 | tf_op jit(solution)/shard_map/ppermute | solution.py:19
  110.8 7.9 %collective-permute-start.14 = (bf16[2,48,1024]{2,1,0:T(8,128)(2,1)S(1)}, bf16[2,48,1024]{2,1,0:T(8,128)(2,1)S(1)}, u32[]{:S(2)}, u32[]{:S(2)}) collective-permute-start(bf16[2,48,1024]{2,1,0:T(8,128)(2,1)S(1)} %collective-permute-done.12), channel_id=1, source_target_pairs={{0,8},{8,16},{16,24},{24,32},{32,40},{40,48},{48,56},{56,64},{64,7... | collective-permute-start | bytes 589832 | tf_op jit(solution)/shard_map/ppermute | solution.py:16
  145.0 12.4 %copy-start.5 = (s32[2]{0:T(128)S(1)}, s32[2]{0:T(128)}, u32[]{:S(2)}) copy-start(s32[2]{0:T(128)} %param.18) | copy-start | bytes 28
  161.6 2.0 copy-start.1
  190.5 2.4 copy-start
  225.2 16.6 %all-to-all-start.2 = ((f32[8,1,768]{2,1,0:T(1,128)}), f32[8,1,768]{2,1,0:T(1,128)S(1)}, u32[]{:S(2)}, u32[]{:S(2)}) async-start(f32[8,1,768]{2,1,0:T(1,128)} %reshape.139), calls=%async_computation.2 | async-start | bytes 49152 | tf_op jit(solution)/shard_map/all_to_all | solution.py:138
  241.8 10.0 %all-to-all-start = ((f32[8,1,768]{2,1,0:T(1,128)}), f32[8,1,768]{2,1,0:T(1,128)S(1)}, u32[]{:S(2)}, u32[]{:S(2)}) async-start(f32[8,1,768]{2,1,0:T(1,128)} %reshape.137), calls=%async_computation | async-start | bytes 49152 | tf_op jit(solution)/shard_map/all_to_all | solution.py:137
  251.8 4.9 %copy-start.4 = (bf16[2,48,256]{2,1,0:T(8,128)(2,1)S(1)}, bf16[2,48,256]{2,1,0:T(8,128)(2,1)}, u32[]{:S(2)}) copy-start(bf16[2,48,256]{2,1,0:T(8,128)(2,1)} %param.16) | copy-start | bytes 147460
  251.8 4.9 %copy-start.6 = (s32[2,8]{1,0:T(2,128)S(1)}, s32[2,8]{1,0:T(2,128)}, u32[]{:S(2)}) copy-start(s32[2,8]{1,0:T(2,128)} %param.21) | copy-start | bytes 196
  251.8 42.4 %all-to-all-start.1 = ((f32[1,96,8192]{2,0,1:T(1,128)}), f32[1,96,8192]{2,0,1:T(1,128)S(1)}, u32[]{:S(2)}, u32[]{:S(2)}) async-start(f32[1,96,8192]{2,0,1:T(1,128)} %copy.84), calls=%async_computation.1 | async-start | bytes 6291456 | tf_op jit(solution)/shard_map/all_to_all | solution.py:136
Sparse Core Ops, SparseCore 0:
  119.6 27.2 all-gather.1
